TPU v7x, 512 devices: a whole 4x4x16 slice. The times are simulated.
512 devices in a mesh: row: 16 (over z), col: 32 (over y, x, core).
Axes of the slice: x: 4, y: 4, z: 16, core: 2. Of those that a mesh axis runs over, the one named last changes fastest.
Arguments:
- inputs: bfloat16 [2048, 8192], P('col', 'row'), may hold values from -6 to 6
- gate_pre: bfloat16 [2048, 14784], P('row', 'col'), may hold values from -6 to 6
- up_pre: bfloat16 [2048, 14784], P('row', 'col'), may hold values from -6 to 6
- w_gate: bfloat16 [8192, 14784], P('row', 'col'), may hold values from -0.0625 to 0.0625
- w_up: bfloat16 [8192, 14784], P('row', 'col'), may hold values from -0.0625 to 0.0625
- w_down: bfloat16 [14784, 8192], P('col', 'row'), may hold values from -0.046875 to 0.046875
- grad_out: bfloat16 [2048, 8192], P('col', 'row'), may hold values from -1.5 to 1.5
Outputs:
- grad_in: bfloat16 [2048, 8192], P('col', 'row')
- grad_gate: bfloat16 [8192, 14784], P('row', 'col')
- grad_up: bfloat16 [8192, 14784], P('row', 'col')
- grad_down: bfloat16 [14784, 8192], P('col', 'row')
All inputs are finite; a program needn't handle non-finite values.
Results may differ from a plain program's by a relative error of at most 0.025.
Values may be sent and summed in bfloat16 or wider, within the bound.
No kernel may reach another device: no remote copies, remote signals or barrier semaphores. Data moves between devices by JAX's collectives and lax.ppermute only.
A program may use at most 64 MiB of HBM per device.

v0:
```python
import jax
import jax.numpy as jnp
from jax import lax
from jax.sharding import PartitionSpec as P


def contract_rows(left, right):
    return lax.dot_general(
        left, right, (((0,), (0,)), ((), ())), preferred_element_type=jnp.float32
    )


def contract_cols(left, right):
    return lax.dot_general(
        left, right, (((1,), (1,)), ((), ())), preferred_element_type=jnp.float32
    )


def pointwise(gate_pre, up_pre, hidden_grad):
    gate_value = gate_pre.astype(jnp.float32)
    up_value = up_pre.astype(jnp.float32)
    sigmoid_gate = jax.nn.sigmoid(gate_value)
    activated = gate_value * sigmoid_gate
    hidden = (activated * up_value).astype(jnp.bfloat16)
    up_grad = (hidden_grad * activated).astype(jnp.bfloat16)
    gate_grad = (
        hidden_grad * up_value * sigmoid_gate * (1.0 + gate_value * (1.0 - sigmoid_gate))
    ).astype(jnp.bfloat16)
    return (hidden, gate_grad, up_grad)


def shards(inputs, gate_pre, up_pre, w_gate, w_up, w_down, grad_out):
    all_grad_out, all_inputs = (
        lax.all_gather(grad_out, "col", axis=0, tiled=True),
        lax.all_gather(inputs, "col", axis=0, tiled=True),
    )
    hidden_grad = lax.psum_scatter(
        contract_cols(all_grad_out, w_down).astype(jnp.bfloat16),
        "row",
        scatter_dimension=0,
        tiled=True,
    ).astype(jnp.float32)
    share_hidden, share_gate, share_up = pointwise(gate_pre, up_pre, hidden_grad)
    hidden, gate_grad, up_grad = (
        lax.all_gather(share_hidden, "row", axis=0, tiled=True),
        lax.all_gather(share_gate, "row", axis=0, tiled=True),
        lax.all_gather(share_up, "row", axis=0, tiled=True),
    )
    grad_down = contract_rows(hidden, all_grad_out).astype(jnp.bfloat16)
    grad_gate = contract_rows(all_inputs, gate_grad).astype(jnp.bfloat16)
    grad_up = contract_rows(all_inputs, up_grad).astype(jnp.bfloat16)
    grad_in = lax.psum_scatter(
        (contract_cols(gate_grad, w_gate) + contract_cols(up_grad, w_up)).astype(jnp.bfloat16),
        "col",
        scatter_dimension=0,
        tiled=True,
    )
    return (grad_in, grad_gate, grad_up, grad_down)


def solution(mesh):
    return jax.shard_map(
        shards,
        mesh=mesh,
        in_specs=(
            P("col", "row"),
            P("row", "col"),
            P("row", "col"),
            P("row", "col"),
            P("row", "col"),
            P("col", "row"),
            P("col", "row"),
        ),
        out_specs=(P("col", "row"), P("row", "col"), P("row", "col"), P("col", "row")),
        check_vma=False,
    )
```

profile of v0, /device:TPU:2, one launch (start us, length us, event | category | flops | bytes accessed | tf_op | source)
XLA Modules:
  0.0 553.4 jit_solution(13441405227481804049)
XLA Ops:
  7.2 0.0 copy-start
  7.2 0.0 all-gather.6.cloned.1.call-start
  7.2 0.7 all-gather.6.cloned.1.call-update
  7.9 0.0 reduce-scatter.7.cloned.1.call-start
  8.0 66.2 %all-gather.6.cloned.1.call-done = bf16[2048,512]{1,0:T(8,128)(2,1)} async-done(((bf16[64,512]{1,0:T(8,128)(2,1)}), bf16[2048,512]{1,0:T(8,128)(2,1)}) %all-gather.6.cloned.1.call-update) | async-done | bytes 2097168 | tf_op jit(solution)/shard_map/all_gather | solution.py:34
  74.2 2.8 convolution_convert_fusion
  77.0 2.5 copy.11
  79.5 0.0 copy-start.3
  79.5 0.0 copy-start.4
  79.5 0.0 reduce-scatter.7.cloned.1.call-update
  79.5 0.0 all-gather.8.cloned.1.call-start
  79.6 73.9 %reduce-scatter.7.cloned.1.call-done = bf16[128,462]{1,0:T(8,128)(2,1)} async-done(((bf16[2048,462]{1,0:T(8,128)(2,1)}), bf16[128,462]{1,0:T(8,128)(2,1)}) %reduce-scatter.7.cloned.1.call-update) | async-done | bytes 118288
  153.5 1.0 copy.12
  154.5 0.0 copy-done.3
  154.5 0.0 copy-done.4
  154.5 0.9 fusion.6
  155.4 0.0 all-gather.8.cloned.1.call-update
  155.4 0.0 all-gather.10.cloned.1.call-start
  155.5 0.5 all-gather.10.cloned.1.call-update
  156.0 0.0 all-gather.12.cloned.1.call-start
  156.0 0.5 all-gather.12.cloned.1.call-update
  156.6 0.0 all-gather.14.cloned.1.call-start
  156.6 0.5 all-gather.14.cloned.1.call-update
  157.1 0.0 copy-start.2
  157.2 0.0 reduce-scatter.5.cloned.1.call-start
  157.2 73.9 %all-gather.8.cloned.1.call-done = bf16[2048,462]{0,1:T(8,128)(2,1)} async-done(((bf16[128,462]{0,1:T(8,128)(2,1)}), bf16[2048,462]{0,1:T(8,128)(2,1)}) %all-gather.8.cloned.1.call-update) | async-done | bytes 1892368 | tf_op jit(solution)/shard_map/all_gather | solution.py:46
  231.1 0.0 copy-done
  231.1 4.8 fusion.11
  235.8 71.0 %all-gather.10.cloned.1.call-done = bf16[2048,462]{0,1:T(8,128)(2,1)} async-done(((bf16[128,462]{0,1:T(8,128)(2,1)}), bf16[2048,462]{0,1:T(8,128)(2,1)}) %all-gather.10.cloned.1.call-update) | async-done | bytes 1892368 | tf_op jit(solution)/shard_map/all_gather | solution.py:47
  306.8 0.0 copy-done.2
  306.8 5.5 add_convert_fusion
  312.3 0.0 reduce-scatter.5.cloned.1.call-update
  312.3 0.0 copy-start.1
  312.3 51.9 %all-gather.12.cloned.1.call-done = bf16[2048,512]{1,0:T(8,128)(2,1)} async-done(((bf16[64,512]{1,0:T(8,128)(2,1)}), bf16[2048,512]{1,0:T(8,128)(2,1)}) %all-gather.12.cloned.1.call-update) | async-done | bytes 2097168 | tf_op jit(solution)/shard_map/all_gather | solution.py:35
  364.3 0.0 copy-start.5
  364.3 4.2 fusion.1
  368.5 0.0 copy-done.1
  368.5 0.0 copy-done.5
  368.5 1.9 fusion
  370.4 73.5 %all-gather.14.cloned.1.call-done = bf16[2048,462]{0,1:T(8,128)(2,1)} async-done(((bf16[128,462]{0,1:T(8,128)(2,1)}), bf16[2048,462]{0,1:T(8,128)(2,1)}) %all-gather.14.cloned.1.call-update) | async-done | bytes 1892368 | tf_op jit(solution)/shard_map/all_gather | solution.py:45
  444.0 4.1 convolution_convert_fusion.1
  448.0 98.5 %reduce-scatter.5.cloned.1.call-done = bf16[64,512]{1,0:T(8,128)(2,1)} async-done(((bf16[2048,512]{1,0:T(8,128)(2,1)}), bf16[64,512]{1,0:T(8,128)(2,1)}) %reduce-scatter.5.cloned.1.call-update) | async-done | bytes 65552 | tf_op jit(solution)/shard_map/reduce_scatter | solution.py:52
Async XLA Ops:
  7.2 223.9 %copy-start = (bf16[512,462]{0,1:T(8,128)(2,1)S(1)}, bf16[512,462]{0,1:T(8,128)(2,1)}, u32[]{:S(2)}) copy-start(bf16[512,462]{0,1:T(8,128)(2,1)} %param.10) | copy-start | bytes 1419268
  7.2 67.0 %all-gather.6.cloned.1.call-start = ((), (), s32[]{:S(2)}) async-start(), calls=%async_computation.2 | async-start | bytes 2162688 | tf_op jit(solution)/shard_map/all_gather | solution.py:34
  7.9 145.5 %reduce-scatter.7.cloned.1.call-start = ((), (), s32[]{:S(2)}) async-start(), calls=%async_computation.8 | async-start | bytes 2228224
  79.5 75.0 %copy-start.3 = (bf16[128,462]{0,1:T(8,128)(2,1)S(1)}, bf16[128,462]{0,1:T(8,128)(2,1)}, u32[]{:S(2)}) copy-start(bf16[128,462]{0,1:T(8,128)(2,1)} %param.9) | copy-start | bytes 354820
  79.5 75.0 %copy-start.4 = (bf16[128,462]{0,1:T(8,128)(2,1)S(1)}, bf16[128,462]{0,1:T(8,128)(2,1)}, u32[]{:S(2)}) copy-start(bf16[128,462]{0,1:T(8,128)(2,1)} %param.8) | copy-start | bytes 354820
  79.5 151.6 %all-gather.8.cloned.1.call-start = ((), (), s32[]{:S(2)}) async-start(), calls=%async_computation.3 | async-start | bytes 2019328 | tf_op jit(solution)/shard_map/all_gather | solution.py:46
  155.4 151.4 %all-gather.10.cloned.1.call-start = ((), (), s32[]{:S(2)}) async-start(), calls=%async_computation.4 | async-start | bytes 2019328 | tf_op jit(solution)/shard_map/all_gather | solution.py:47
  156.0 208.3 %all-gather.12.cloned.1.call-start = ((), (), s32[]{:S(2)}) async-start(), calls=%async_computation.6 | async-start | bytes 2162688 | tf_op jit(solution)/shard_map/all_gather | solution.py:35
  156.6 287.4 %all-gather.14.cloned.1.call-start = ((), (), s32[]{:S(2)}) async-start(), calls=%async_computation.7 | async-start | bytes 2019328 | tf_op jit(solution)/shard_map/all_gather | solution.py:45
  157.1 149.7 %copy-start.2 = (bf16[512,462]{0,1:T(8,128)(2,1)S(1)}, bf16[512,462]{0,1:T(8,128)(2,1)}, u32[]{:S(2)}) copy-start(bf16[512,462]{0,1:T(8,128)(2,1)} %param.11) | copy-start | bytes 1419268
  157.2 389.4 %reduce-scatter.5.cloned.1.call-start = ((), (), s32[]{:S(2)}) async-start(), calls=%async_computation.5 | async-start | bytes 2162688 | tf_op jit(solution)/shard_map/reduce_scatter | solution.py:52
  312.3 56.2 %copy-start.1 = (bf16[2048,462]{0,1:T(8,128)(2,1)S(1)}, bf16[2048,462]{0,1:T(8,128)(2,1)}, u32[]{:S(2)}) copy-start(bf16[2048,462]{0,1:T(8,128)(2,1)} %all-gather.8.cloned.1.call-done) | copy-start | bytes 5677060
  364.3 4.2 copy-start.5
Sparse Core Ops, SparseCore 0:
  11.1 63.0 all-gather.5
  79.6 73.7 reduce-scatter.6
  156.0 74.9 all-gather.7
  233.5 73.2 all-gather.9
  309.8 54.3 all-gather.11
  366.7 77.2 all-gather.13
  448.9 97.5 reduce-scatter.4
where the time goes:
time: 554 us; the launch traced here: 553 us
  waiting for transfers between devices  511 us (92%)
  matrix products  23.3 us (4%)
  between operations  14.2 us (3%)
    reduce_scatter x1, waiting for transfers between devices, shards(): lax.psum_scatter((contract_cols(gate_grad, w_gate) + contract_cols(up_gra...  98.5 us
    unnamed x8, waiting for transfers between devices  76.2 us
    all_gather x1, waiting for transfers between devices, shards(): lax.all_gather(share_gate, 'row', axis=0, tiled=True)  73.9 us
    all_gather x1, waiting for transfers between devices, shards(): lax.all_gather(share_hidden, 'row', axis=0, tiled=True)  73.5 us
    all_gather x1, waiting for transfers between devices, shards(): lax.all_gather(share_up, 'row', axis=0, tiled=True)  71 us
    all_gather x1, waiting for transfers between devices, shards(): lax.all_gather(grad_out, 'col', axis=0, tiled=True)  66.2 us
    all_gather x1, waiting for transfers between devices, shards(): lax.all_gather(inputs, 'col', axis=0, tiled=True)  51.9 us
    dot_general x3, matrix products, contract_cols(): lax.dot_general(left, right, (((1,), (1,)), ((), ())), preferred_element_...  13.1 us
  transfers between devices with their start and end apart: 7, of which 7 were waited for; matrix products, arithmetic and copies ran while one was open for 4% of the time, Pallas kernels for 0%

commit v1 on v0

--- a/solution.py
+++ b/solution.py
@@ -31,7 +31,9 @@
 
 def shards(inputs, gate_pre, up_pre, w_gate, w_up, w_down, grad_out):
     all_grad_out, all_inputs = (
-        lax.all_gather(grad_out, "col", axis=0, tiled=True),
+        jnp.concatenate(
+            lax.all_to_all(jnp.stack([grad_out] * lax.axis_size("col")), "col", 0, 0), axis=0
+        ),
         lax.all_gather(inputs, "col", axis=0, tiled=True),
     )
     hidden_grad = lax.psum_scatter(

time: 554 us -> 524 us (0.946)
  waiting for transfers between devices: 511 us -> 445 us
  blocking collectives: 0 us -> 36 us
    all_gather x1 -> x0, waiting for transfers between devices: 66.2 us -> none  [shards(): lax.all_gather(grad_out, 'col', axis=0, tiled=True)]
    all_to_all x0 -> x1, blocking collectives: none -> 36 us  [shards(): lax.all_to_all(jnp.stack([grad_out] * lax.axis_size('col')), 'col', 0, 0)]
    unnamed x8 -> x7, waiting for transfers between devices: 76.2 us -> 76.4 us
  transfers between devices with their start and end apart: 7 -> 6, of which waited for: 7 -> 6; matrix products, arithmetic and copies ran while one was open for 4% -> 4% of each run, Pallas kernels for 0% -> 0%
where the time goes in v1:
time: 524 us
  waiting for transfers between devices  445 us (85%)
  blocking collectives  36 us (7%)
  matrix products  21.7 us (4%)
  between operations  14.2 us (3%)
  local copies, waits for them, and re-layouts  5.99 us (1%)
    reduce_scatter x1, waiting for transfers between devices, shards(): lax.psum_scatter((contract_cols(gate_grad, w_gate) + contract_cols(up_gra...  98.4 us
    unnamed x7, waiting for transfers between devices  76.4 us
    all_gather x1, waiting for transfers between devices, shards(): lax.all_gather(share_gate, 'row', axis=0, tiled=True)  73.7 us
    all_gather x1, waiting for transfers between devices, shards(): lax.all_gather(share_hidden, 'row', axis=0, tiled=True)  73.5 us
    all_gather x1, waiting for transfers between devices, shards(): lax.all_gather(share_up, 'row', axis=0, tiled=True)  71.2 us
    all_gather x1, waiting for transfers between devices, shards(): lax.all_gather(inputs, 'col', axis=0, tiled=True)  51.9 us
    all_to_all x1, blocking collectives, shards(): lax.all_to_all(jnp.stack([grad_out] * lax.axis_size('col')), 'col', 0, 0)  36 us
    dot_general x3, matrix products, contract_cols(): lax.dot_general(left, right, (((1,), (1,)), ((), ())), preferred_element_...  11.4 us
  transfers between devices with their start and end apart: 6, of which 6 were waited for; matrix products, arithmetic and copies ran while one was open for 4% of the time, Pallas kernels for 0%

profile of v1, /device:TPU:2, one launch (start us, length us, event | category | flops | bytes accessed | tf_op | source)
XLA Modules:
  0.0 524.0 jit_solution(12223590343705402473)
XLA Ops:
  7.2 0.0 copy-start
  7.2 0.0 reduce-scatter.7.cloned.1.call-start
  7.2 1.1 stack.2
  8.3 0.0 copy-start.7
  8.4 36.0 %all_to_all.5 = bf16[32,64,512]{2,1,0:T(8,128)(2,1)S(1)} all-to-all(bf16[32,64,512]{2,1,0:T(8,128)(2,1)S(1)} %stack.2), channel_id=1, replica_groups=mesh['row'=16,'col'=32] {'col'}, dimensions={0} | all-to-all | bytes 4194304 | tf_op jit(solution)/shard_map/all_to_all | solution.py:35
  44.4 0.0 copy-start.2
  44.4 1.3 copy-done.2
  45.7 0.0 copy-done.7
  45.7 1.2 convolution_convert_fusion
  46.9 2.5 copy.11
  49.4 0.0 copy-start.4
  49.4 0.0 copy-start.5
  49.4 0.0 reduce-scatter.7.cloned.1.call-update
  49.4 0.0 all-gather.5.cloned.1.call-start
  49.5 74.7 %reduce-scatter.7.cloned.1.call-done = bf16[128,462]{1,0:T(8,128)(2,1)} async-done(((bf16[2048,462]{1,0:T(8,128)(2,1)}), bf16[128,462]{1,0:T(8,128)(2,1)}) %reduce-scatter.7.cloned.1.call-update) | async-done | bytes 118288
  124.1 1.0 copy.12
  125.2 0.0 copy-done.4
  125.2 0.0 copy-done.5
  125.2 0.9 fusion.6
  126.0 0.0 all-gather.5.cloned.1.call-update
  126.1 0.0 all-gather.7.cloned.1.call-start
  126.1 0.7 all-gather.7.cloned.1.call-update
  126.8 0.0 all-gather.9.cloned.1.call-start
  126.8 0.5 all-gather.9.cloned.1.call-update
  127.4 0.0 all-gather.11.cloned.1.call-start
  127.4 0.5 all-gather.11.cloned.1.call-update
  128.0 0.0 copy-start.3
  128.0 0.0 reduce-scatter.5.cloned.1.call-start
  128.0 73.7 %all-gather.5.cloned.1.call-done = bf16[2048,462]{0,1:T(8,128)(2,1)} async-done(((bf16[128,462]{0,1:T(8,128)(2,1)}), bf16[2048,462]{0,1:T(8,128)(2,1)}) %all-gather.5.cloned.1.call-update) | async-done | bytes 1892368 | tf_op jit(solution)/shard_map/all_gather | solution.py:48
  201.7 0.0 copy-done
  201.7 4.8 fusion.11
  206.5 71.2 %all-gather.7.cloned.1.call-done = bf16[2048,462]{0,1:T(8,128)(2,1)} async-done(((bf16[128,462]{0,1:T(8,128)(2,1)}), bf16[2048,462]{0,1:T(8,128)(2,1)}) %all-gather.7.cloned.1.call-update) | async-done | bytes 1892368 | tf_op jit(solution)/shard_map/all_gather | solution.py:49
  277.6 0.0 copy-done.3
  277.6 5.5 %add_convert_fusion = bf16[2048,512]{1,0:T(8,128)(2,1)} fusion(f32[2048,512]{1,0:T(8,128)} %fusion.11, bf16[2048,462]{0,1:T(8,128)(2,1)} %all-gather.7.cloned.1.call-done, bf16[512,462]{0,1:T(8,128)(2,1)S(1)} %copy-done.3), kind=kOutput, calls=%fused_computation | convolution fusion | flops 970981376 | bytes 8656896 | tf_op jit(solution)/shard_map/dot_general | solution.py:14
  283.1 0.0 reduce-scatter.5.cloned.1.call-update
  283.1 0.0 copy-start.1
  283.1 51.9 %all-gather.9.cloned.1.call-done = bf16[2048,512]{1,0:T(8,128)(2,1)} async-done(((bf16[64,512]{1,0:T(8,128)(2,1)}), bf16[2048,512]{1,0:T(8,128)(2,1)}) %all-gather.9.cloned.1.call-update) | async-done | bytes 2097168 | tf_op jit(solution)/shard_map/all_gather | solution.py:37
  335.1 0.0 copy-start.6
  335.1 4.2 fusion.1
  339.3 0.0 copy-done.1
  339.3 0.0 copy-done.6
  339.3 1.9 fusion
  341.2 73.5 %all-gather.11.cloned.1.call-done = bf16[2048,462]{0,1:T(8,128)(2,1)} async-done(((bf16[128,462]{0,1:T(8,128)(2,1)}), bf16[2048,462]{0,1:T(8,128)(2,1)}) %all-gather.11.cloned.1.call-update) | async-done | bytes 1892368 | tf_op jit(solution)/shard_map/all_gather | solution.py:47
  414.7 4.1 convolution_convert_fusion.1
  418.8 98.4 %reduce-scatter.5.cloned.1.call-done = bf16[64,512]{1,0:T(8,128)(2,1)} async-done(((bf16[2048,512]{1,0:T(8,128)(2,1)}), bf16[64,512]{1,0:T(8,128)(2,1)}) %reduce-scatter.5.cloned.1.call-update) | async-done | bytes 65552 | tf_op jit(solution)/shard_map/reduce_scatter | solution.py:54
Async XLA Ops:
  7.2 194.6 %copy-start = (bf16[512,462]{0,1:T(8,128)(2,1)S(1)}, bf16[512,462]{0,1:T(8,128)(2,1)}, u32[]{:S(2)}) copy-start(bf16[512,462]{0,1:T(8,128)(2,1)} %param.10) | copy-start | bytes 1419268
  7.2 116.9 %reduce-scatter.7.cloned.1.call-start = ((), (), s32[]{:S(2)}) async-start(), calls=%async_computation.8 | async-start | bytes 2228224
  8.3 37.4 %copy-start.7 = (bf16[462,512]{1,0:T(8,128)(2,1)S(1)}, bf16[462,512]{1,0:T(8,128)(2,1)}, u32[]{:S(2)}) copy-start(bf16[462,512]{1,0:T(8,128)(2,1)} %param.12) | copy-start | bytes 1419268
  44.4 1.3 copy-start.2
  49.4 75.8 %copy-start.4 = (bf16[128,462]{0,1:T(8,128)(2,1)S(1)}, bf16[128,462]{0,1:T(8,128)(2,1)}, u32[]{:S(2)}) copy-start(bf16[128,462]{0,1:T(8,128)(2,1)} %param.9) | copy-start | bytes 354820
  49.4 75.8 %copy-start.5 = (bf16[128,462]{0,1:T(8,128)(2,1)S(1)}, bf16[128,462]{0,1:T(8,128)(2,1)}, u32[]{:S(2)}) copy-start(bf16[128,462]{0,1:T(8,128)(2,1)} %param.8) | copy-start | bytes 354820
  49.4 152.3 %all-gather.5.cloned.1.call-start = ((), (), s32[]{:S(2)}) async-start(), calls=%async_computation.3 | async-start | bytes 2019328 | tf_op jit(solution)/shard_map/all_gather | solution.py:48
  126.1 151.6 %all-gather.7.cloned.1.call-start = ((), (), s32[]{:S(2)}) async-start(), calls=%async_computation.4 | async-start | bytes 2019328 | tf_op jit(solution)/shard_map/all_gather | solution.py:49
  126.8 208.3 %all-gather.9.cloned.1.call-start = ((), (), s32[]{:S(2)}) async-start(), calls=%async_computation.6 | async-start | bytes 2162688 | tf_op jit(solution)/shard_map/all_gather | solution.py:37
  127.4 287.4 %all-gather.11.cloned.1.call-start = ((), (), s32[]{:S(2)}) async-start(), calls=%async_computation.7 | async-start | bytes 2019328 | tf_op jit(solution)/shard_map/all_gather | solution.py:47
  128.0 149.7 %copy-start.3 = (bf16[512,462]{0,1:T(8,128)(2,1)S(1)}, bf16[512,462]{0,1:T(8,128)(2,1)}, u32[]{:S(2)}) copy-start(bf16[512,462]{0,1:T(8,128)(2,1)} %param.11) | copy-start | bytes 1419268
  128.0 389.2 %reduce-scatter.5.cloned.1.call-start = ((), (), s32[]{:S(2)}) async-start(), calls=%async_computation.5 | async-start | bytes 2162688 | tf_op jit(solution)/shard_map/reduce_scatter | solution.py:54
  283.1 56.2 %copy-start.1 = (bf16[2048,462]{0,1:T(8,128)(2,1)S(1)}, bf16[2048,462]{0,1:T(8,128)(2,1)}, u32[]{:S(2)}) copy-start(bf16[2048,462]{0,1:T(8,128)(2,1)} %all-gather.5.cloned.1.call-done) | copy-start | bytes 5677060
  335.1 4.2 copy-start.6
Sparse Core Ops, SparseCore 0:
  49.5 74.5 reduce-scatter.6
  126.7 74.9 all-gather.4
  204.3 73.2 all-gather.6
  280.6 54.3 all-gather.8
  337.5 77.2 all-gather.10
  419.6 97.5 reduce-scatter.4
